TPU v7x, 256 devices: a whole 4x4x8 slice. The times are simulated.
256 devices in a mesh: cfg: 2 (over core), req: 8 (over z), seq: 16 (over y, x).
Axes of the slice: x: 4, y: 4, z: 8, core: 2. Of those that a mesh axis runs over, the one named last changes fastest.
Arguments:
- img_hidden: bfloat16 [2, 16, 512, 1536], P('cfg', 'req', 'seq'), may hold values from -6 to 6
- txt_hidden: bfloat16 [2, 16, 160, 1536], P('cfg', 'req', 'seq'), may hold values from -6 to 6
- text_len: int32 [2, 16], P('cfg'), may hold values from 1 to 154, as said below
- pooled: float32 [2, 16, 1536], P('cfg'), may hold values from -6 to 6
- timestep: int32 [16], replicated, may hold values from 0 to 27
- latent: float32 [16, 512, 64], P('req', 'seq', 'cfg'), may hold values from -24 to 24
- mod_weight: bfloat16 [1536, 15360], P(None, ('req', 'seq')), may hold values from -0.15625 to 0.15625
- mod_bias: float32 [15360], P(('req', 'seq')), may hold values from -2 to 2
- img_qkv: bfloat16 [1536, 3, 1536], P(None, None, 'req'), may hold values from -2.5 to 2.5
- txt_kv: bfloat16 [1536, 2, 1536], P(None, None, 'req'), may hold values from -0.15625 to 0.15625
- out_weight: bfloat16 [1536, 1536], P('req'), may hold values from -0.15625 to 0.15625
- fc_in: bfloat16 [1536, 6144], P(None, 'seq'), may hold values from -0.15625 to 0.15625
- fc_out: bfloat16 [6144, 1536], P('seq'), may hold values from -0.078125 to 0.078125
- final_weight: bfloat16 [1536, 64], replicated, may hold values from -0.15625 to 0.15625
Outputs:
- velocity: float32 [16, 512, 64], P('req', 'seq', 'cfg')
- next_latent: float32 [16, 512, 64], P('req', 'seq', 'cfg')
- latent_norm: float32 [16], P('req')
- latent_peak: float32 [16], P('req')
Inputs may be any that keep to these rules, and one draw needn't show every extreme that they name: Text slots from text_len to 159 of a request are padding; every draw has a request of length 154 and one of length 1.
All inputs are finite; a program needn't handle non-finite values.
Results may differ from a plain program's by a relative error of at most 0.015.
Values may be sent and summed in bfloat16 or wider, within the bound.
No kernel may reach another device: no remote copies, remote signals or barrier semaphores. Data moves between devices by JAX's collectives and lax.ppermute only.
A program may use at most 64 MiB of HBM per device.

v0:
```python
import math
import jax
import jax.numpy as jnp
from jax import lax
from jax.sharding import PartitionSpec as P

D = 1536
HD = 64
PATCHC = 64
IMG = 512
STEPS = 28
SIGMA_SHIFT = 3.0
GUIDANCE = 5.0
EPSILON = 1e-06
MASKED_SCORE = -1e30


def from_partner(value, axis, distance):
    mask = 2**distance
    pairs = [(source, source ^ mask) for source in range(lax.axis_size(axis))]
    return lax.ppermute(value, axis, pairs)


def shifted(fraction):
    return SIGMA_SHIFT * fraction / (1.0 + (SIGMA_SHIFT - 1.0) * fraction)


def plan(timestep):
    position = timestep.astype(jnp.float32)
    return (shifted(1.0 - position / STEPS), shifted(1.0 - (position + 1.0) / STEPS))


def time_features(sigma):
    half_width = D // 2
    frequency = jnp.exp(-math.log(10000.0) * jnp.arange(half_width, dtype=jnp.float32) / half_width)
    angles = (1000.0 * sigma)[:, None] * frequency[None, :]
    return jnp.concatenate([jnp.cos(angles), jnp.sin(angles)], axis=1)


def layer_norm(values):
    average = jnp.mean(values, axis=-1, keepdims=True)
    centred = values - average
    spread = jnp.mean(centred * centred, axis=-1, keepdims=True)
    return centred * lax.rsqrt(spread + EPSILON)


def attention(queries, key_rows, value_rows, live_keys):
    query_count = queries.shape[0]
    head_count = queries.shape[1]
    block_rows = min(512, query_count)
    scale_factor = HD ** (-0.5)

    def one_block(query_block):
        scores = (
            jnp.einsum("qhd,khd->hqk", query_block, key_rows, preferred_element_type=jnp.float32)
            * scale_factor
        )
        scores = jnp.where(live_keys[None, None, :], scores, MASKED_SCORE)
        highest = jnp.max(scores, axis=-1, keepdims=True)
        exp_scores = jnp.exp(scores - highest)
        weights = (exp_scores / jnp.sum(exp_scores, axis=-1, keepdims=True)).astype(jnp.bfloat16)
        mixture = jnp.einsum(
            "hqk,khd->qhd", weights, value_rows, preferred_element_type=jnp.float32
        )
        return mixture.astype(jnp.bfloat16)

    blocks = queries.reshape(query_count // block_rows, block_rows, head_count, HD)
    return lax.map(one_block, blocks).reshape(query_count, head_count * HD)


def on_device(
    img_hidden,
    txt_hidden,
    text_len,
    pooled,
    timestep,
    latent,
    mod_weight,
    mod_bias,
    img_qkv,
    txt_kv,
    out_weight,
    fc_in,
    fc_out,
    final_weight,
):
    group_size = img_hidden.shape[1]
    current, upcoming = plan(timestep)
    activated = jax.nn.silu(pooled[0] + time_features(current)).astype(jnp.bfloat16)
    columns = jnp.dot(activated, mod_weight, preferred_element_type=jnp.float32) + mod_bias
    every_mod = lax.all_gather(columns, ("req", "seq"), axis=1, tiled=True)
    offset = lax.axis_index("req") * group_size
    modulation = lax.dynamic_slice_in_dim(every_mod, offset, group_size, 0).reshape(
        group_size, 10, 1, D
    )
    shift_attn, scale_attn, gate_attn = (modulation[:, 0], modulation[:, 1], modulation[:, 2])
    shift_mlp, scale_mlp, gate_mlp = (modulation[:, 3], modulation[:, 4], modulation[:, 5])
    shift_text, scale_text = (modulation[:, 6], modulation[:, 7])
    scale_final, shift_final = (modulation[:, 8], modulation[:, 9])
    img_float = img_hidden[0].astype(jnp.float32)
    img_in = (layer_norm(img_float) * (1.0 + scale_attn) + shift_attn).astype(jnp.bfloat16)
    txt_in = (
        layer_norm(txt_hidden[0].astype(jnp.float32)) * (1.0 + scale_text) + shift_text
    ).astype(jnp.bfloat16)
    all_img, all_txt = (
        lax.all_gather(img_in, "req", axis=0, tiled=True),
        lax.all_gather(txt_in, "req", axis=0, tiled=True),
    )
    head_width = img_qkv.shape[2]
    local_heads = head_width // HD
    qkv_columns = img_qkv.reshape(D, 3 * head_width)
    kv_columns = txt_kv.reshape(D, 2 * head_width)
    own_img, own_txt = (
        lax.all_to_all(all_img, "seq", split_axis=0, concat_axis=1, tiled=True),
        lax.all_to_all(all_txt, "seq", split_axis=0, concat_axis=1, tiled=True),
    )
    own_proj = jnp.einsum(
        "rnd,dc->rnc", own_img, qkv_columns, preferred_element_type=jnp.float32
    ).astype(jnp.bfloat16)
    own_proj_txt = jnp.einsum(
        "rnd,dc->rnc", own_txt, kv_columns, preferred_element_type=jnp.float32
    ).astype(jnp.bfloat16)
    local_count = own_proj.shape[0]
    image_rows = own_proj.shape[1]
    text_rows = own_proj_txt.shape[1]
    first_request = lax.axis_index("seq") * local_count

    def attend_request(operands):
        projected, projected_txt, request_slot = operands
        queries = projected[:, :head_width]
        key_rows = jnp.concatenate(
            [projected[:, head_width : 2 * head_width], projected_txt[:, :head_width]], axis=0
        )
        value_rows = jnp.concatenate(
            [projected[:, 2 * head_width :], projected_txt[:, head_width:]], axis=0
        )
        text_count = lax.dynamic_index_in_dim(text_len[0], first_request + request_slot, 0, False)
        live_keys = jnp.arange(image_rows + text_rows, dtype=jnp.int32) < image_rows + text_count
        total_keys = image_rows + text_rows
        return attention(
            queries.reshape(image_rows, local_heads, HD),
            key_rows.reshape(total_keys, local_heads, HD),
            value_rows.reshape(total_keys, local_heads, HD),
            live_keys,
        )

    attended = lax.map(
        attend_request, (own_proj, own_proj_txt, jnp.arange(local_count, dtype=jnp.int32))
    )
    projected_rows = jnp.einsum(
        "rnk,kd->rnd", attended, out_weight, preferred_element_type=jnp.float32
    )
    moved_rows = lax.all_to_all(
        projected_rows.astype(jnp.bfloat16), "seq", split_axis=1, concat_axis=0, tiled=True
    ).astype(projected_rows.dtype)
    attn_out = lax.psum_scatter(
        moved_rows.astype(jnp.bfloat16), "req", scatter_dimension=0, tiled=True
    ).astype(jnp.float32)
    img_mid = img_float + gate_attn * attn_out
    mlp_in = (layer_norm(img_mid) * (1.0 + scale_mlp) + shift_mlp).astype(jnp.bfloat16)
    raised = jnp.einsum(
        "rnd,df->rnf",
        lax.all_gather(mlp_in, "seq", axis=1, tiled=True),
        fc_in,
        preferred_element_type=jnp.float32,
    )
    hidden = jax.nn.gelu(raised, approximate=True).astype(jnp.bfloat16)
    mlp_terms = jnp.einsum("rnf,fd->rnd", hidden, fc_out, preferred_element_type=jnp.float32)
    mlp_out = lax.psum_scatter(
        mlp_terms.astype(jnp.bfloat16), "seq", scatter_dimension=1, tiled=True
    ).astype(jnp.float32)
    img_out = img_mid + gate_mlp * mlp_out
    final_in = (layer_norm(img_out) * (1.0 + scale_final) + shift_final).astype(jnp.bfloat16)
    own_velocity = jnp.einsum(
        "rnd,dc->rnc", final_in, final_weight, preferred_element_type=jnp.float32
    )
    half_values = latent.shape[2]
    half_index = lax.axis_index("cfg")
    kept_velocity = lax.dynamic_slice_in_dim(own_velocity, half_index * half_values, half_values, 2)
    sent_velocity = lax.dynamic_slice_in_dim(
        own_velocity, (1 - half_index) * half_values, half_values, 2
    )
    other_velocity = from_partner(sent_velocity, "cfg", 0)
    cond_first = half_index == 0
    conditional = jnp.where(cond_first, kept_velocity, other_velocity)
    unconditional = jnp.where(cond_first, other_velocity, kept_velocity)
    guided = unconditional + GUIDANCE * (conditional - unconditional)
    step_size = lax.dynamic_slice_in_dim(upcoming - current, offset, group_size, 0)
    next_latent = latent + step_size[:, None, None] * guided
    squares = jnp.sum(next_latent * next_latent, axis=(1, 2))
    largest = jnp.max(jnp.abs(next_latent), axis=(1, 2))
    square_total = lax.psum(squares, ("cfg", "seq"))
    peak_value = lax.pmax(largest, ("cfg", "seq"))
    latent_norm = jnp.sqrt(square_total / (IMG * PATCHC))
    return (guided, next_latent, latent_norm, peak_value)


def solution(mesh):
    placed = (
        P("cfg", "req", "seq", None),
        P("cfg", "req", "seq", None),
        P("cfg", None),
        P("cfg", None, None),
        P(),
        P("req", "seq", "cfg"),
        P(None, ("req", "seq")),
        P(("req", "seq")),
        P(None, None, "req"),
        P(None, None, "req"),
        P("req", None),
        P(None, "seq"),
        P("seq", None),
        P(),
    )
    return jax.shard_map(
        on_device,
        mesh=mesh,
        in_specs=placed,
        out_specs=(P("req", "seq", "cfg"), P("req", "seq", "cfg"), P("req"), P("req")),
        check_vma=False,
    )
```

profile of v0, /device:TPU:1, one launch (start us, length us, event | category | flops | bytes accessed | tf_op | source)
XLA Modules:
  0.0 808.6 jit_solution(5461950614559532431)
XLA Ops:
  7.2 0.8 divide_subtract_fusion
  8.0 0.3 multiply_cosine_fusion
  8.3 1.2 fusion.18
  9.5 299.6 %all-gather = f32[128,120,16]{1,2,0:T(8,128)S(1)} all-gather(f32[1,120,16]{1,2,0:T(8,128)S(1)} %fusion.18), channel_id=1, replica_groups=mesh['cfg'=2,'req'=8,'seq'=16] {'req','seq'}, dimensions={0}, use_global_device_ids=true | all-gather | bytes 990720 | tf_op jit(solution)/shard_map/all_gather | solution.py:91
  309.1 0.3 copy.26
  309.4 1.6 reshape.180
  311.0 1.1 dynamic-slice_bitcast_fusion
  312.2 0.7 fusion.60
  313.0 0.2 fusion.31
  313.3 0.8 fusion.34
  314.5 19.9 %all_gather.14 = bf16[16,10,1536]{2,1,0:T(8,128)(2,1)S(1)} all-gather(bf16[2,10,1536]{2,1,0:T(8,128)(2,1)S(1)} %fusion.42), channel_id=1, replica_groups=mesh['cfg'=2,'req'=8,'seq'=16] {'req'}, dimensions={0}, use_global_device_ids=true | all-gather | bytes 552960 | tf_op jit(solution)/shard_map/all_gather | solution.py:107
  334.4 13.0 %all_to_all.30 = bf16[16,10,1536]{2,1,0:T(8,128)(2,1)S(1)} all-to-all(bf16[16,10,1536]{2,1,0:T(8,128)(2,1)S(1)} %all_gather.14), channel_id=1, replica_groups=mesh['cfg'=2,'req'=8,'seq'=16] {'seq'}, dimensions={0} | all-to-all | bytes 983040 | tf_op jit(solution)/shard_map/all_to_all | solution.py:115
  347.4 51.1 %all-gather.4.cloned.1.call-done = bf16[16,32,1536]{2,1,0:T(8,128)(2,1)} async-done(((bf16[2,32,1536]{2,1,0:T(8,128)(2,1)}), bf16[16,32,1536]{2,1,0:T(8,128)(2,1)}) %all-gather.4.cloned.1.call-update) | async-done | bytes 1572880 | tf_op jit(solution)/shard_map/all_gather | solution.py:106
  398.5 5.8 all-to-all-start
  404.3 0.2 reduce-scatter.3.cloned.1.call-start
  404.6 0.6 fusion.62
  405.2 0.6 iota_compare_fusion
  406.0 1.7 convolution_convert_fusion.3
  407.8 13.1 %all-to-all-done = bf16[16,32,1536]{2,1,0:T(8,128)(2,1)} async-done(((bf16[16,32,1536]{2,1,0:T(8,128)(2,1)}), bf16[16,32,1536]{2,1,0:T(8,128)(2,1)}, u32[]{:S(2)}, u32[]{:S(2)}) %all-to-all-start) | async-done | bytes 1572896 | tf_op jit(solution)/shard_map/all_to_all | solution.py:114
  420.9 2.5 convolution_convert_fusion.2
  423.5 3.5 fusion.63
  427.1 2.7 fusion.17
  429.8 0.6 fusion.2
  430.4 4.1 copy.58
  434.5 0.5 broadcast.203
  435.0 11.5 %reduce.2 = bf16[512,1536]{1,0:T(8,128)(2,1)S(1)} reduce(bf16[512,1,1536]{2,1,0:T(2,128)(2,1)} %bitcast.126, bf16[]{:T(256)} %broadcast.203), dimensions={1}, to_apply=%bitcast.124.reduce_sub_computation | reduce | bytes 3145730
  446.5 2.1 reshape.184
  448.6 18.4 %all_to_all.31 = bf16[16,2,24576]{2,1,0:T(2,128)(2,1)S(1)} all-to-all(bf16[16,2,24576]{2,1,0:T(2,128)(2,1)} %reshape.184), channel_id=1, replica_groups=mesh['cfg'=2,'req'=8,'seq'=16] {'seq'}, dimensions={0} | all-to-all | bytes 3145728 | tf_op jit(solution)/shard_map/all_to_all | solution.py:153
  466.9 6.3 reshape.185
  473.2 3.4 copy.36
  476.6 0.6 copy-done.5
  477.3 42.2 %reduce-scatter.3.cloned.1.call-done = bf16[2,32,1536]{2,1,0:T(8,128)(2,1)} async-done(((bf16[16,32,1536]{2,1,0:T(8,128)(2,1)}), bf16[2,32,1536]{2,1,0:T(8,128)(2,1)}) %reduce-scatter.3.cloned.1.call-update) | async-done | bytes 196624 | tf_op jit(solution)/shard_map/reduce_scatter | solution.py:156
  519.5 1.1 fusion.35
  520.5 1.1 multiply_reduce_fusion.1
  521.7 1.8 add_convert_fusion.1
  523.5 54.8 %all-gather.6.cloned.1.call-done = bf16[2,512,1536]{2,1,0:T(8,128)(2,1)} async-done(((bf16[2,32,1536]{2,1,0:T(8,128)(2,1)}), bf16[2,512,1536]{2,1,0:T(8,128)(2,1)}) %all-gather.6.cloned.1.call-update) | async-done | bytes 3145744 | tf_op jit(solution)/shard_map/all_gather | solution.py:163
  578.4 7.6 convolution_convert_fusion
  586.0 0.6 copy-done.6
  586.6 78.8 %reduce-scatter.5.cloned.1.call-done = bf16[2,32,1536]{2,1,0:T(8,128)(2,1)} async-done(((bf16[2,512,1536]{2,1,0:T(8,128)(2,1)}), bf16[2,32,1536]{2,1,0:T(8,128)(2,1)}) %reduce-scatter.5.cloned.1.call-update) | async-done | bytes 196624 | tf_op jit(solution)/shard_map/reduce_scatter | solution.py:169
  665.5 1.1 fusion.58
  666.6 1.1 multiply_reduce_fusion
  667.8 1.2 fusion.43
  669.1 2.4 collective-permute-start
  671.6 0.8 collective-permute-done
  672.3 0.7 abs_reduce_fusion
  673.1 65.3 %psum.7 = f32[2]{0:T(128)S(1)} all-reduce(f32[2]{0:T(128)S(1)} %get-tuple-element.41), channel_id=1, replica_groups=mesh['cfg'=2,'req'=8,'seq'=16] {'cfg','seq'}, use_global_device_ids=true, to_apply=%region_13.14 | all-reduce | flops 2 | bytes 16 | tf_op jit(solution)/shard_map/psum | solution.py:192
  738.3 0.5 multiply_sqrt_fusion
  738.8 63.2 %pmax.7 = f32[2]{0:T(128)} all-reduce(f32[2]{0:T(128)S(1)} %get-tuple-element.40), channel_id=1, replica_groups=mesh['cfg'=2,'req'=8,'seq'=16] {'cfg','seq'}, use_global_device_ids=true, to_apply=%region_15.16 | all-reduce | flops 2 | bytes 16 | tf_op jit(solution)/shard_map/pmax | solution.py:193
  (61 shorter events, 1.5 us)
Async XLA Ops:
  7.2 413.7 %copy-start = (bf16[1536,3,192]{0,2,1:T(8,128)(2,1)S(1)}, bf16[1536,3,192]{0,2,1:T(8,128)(2,1)}, u32[]{:S(2)}) copy-start(bf16[1536,3,192]{0,2,1:T(8,128)(2,1)} %param.22) | copy-start | bytes 5308420
  7.2 391.3 %all-gather.4.cloned.1.call-start = ((), (), s32[]{:S(2)}) async-start(), calls=%async_computation.5 | async-start | bytes 1769472 | tf_op jit(solution)/shard_map/all_gather | solution.py:106
  309.4 3.5 copy-start.1
  309.4 4.7 copy-start.4
  347.4 57.1 %copy-start.13 = (s32[1,16]{1,0:T(1,128)S(1)}, s32[1,16]{1,0:T(1,128)}, u32[]{:S(2)}) copy-start(s32[1,16]{1,0:T(1,128)} %param.16) | copy-start | bytes 196
  398.5 22.4 %all-to-all-start = ((bf16[16,32,1536]{2,1,0:T(8,128)(2,1)}), bf16[16,32,1536]{2,1,0:T(8,128)(2,1)}, u32[]{:S(2)}, u32[]{:S(2)}) async-start(bf16[16,32,1536]{2,1,0:T(8,128)(2,1)} %all-gather.4.cloned.1.call-done), calls=%async_computation | async-start | bytes 3145728 | tf_op jit(solution)/shard_map/all_to_all | solution.py:114
  404.3 115.1 %reduce-scatter.3.cloned.1.call-start = ((), (), s32[]{:S(2)}) async-start(), calls=%async_computation.6 | async-start | bytes 1769472 | tf_op jit(solution)/shard_map/reduce_scatter | solution.py:156
  427.1 2.7 copy-start.3
  476.5 0.7 copy-start.5
  476.5 0.7 copy-start.8
  476.5 0.7 copy-start.9
  476.5 101.8 %copy-start.11 = (bf16[384,1536]{1,0:T(8,128)(2,1)S(1)}, bf16[384,1536]{1,0:T(8,128)(2,1)}, u32[]{:S(2)}) copy-start(bf16[384,1536]{1,0:T(8,128)(2,1)} %param.26) | copy-start | bytes 3538948
  476.6 101.8 %all-gather.6.cloned.1.call-start = ((), (), s32[]{:S(2)}) async-start(), calls=%async_computation.7 | async-start | bytes 3342336 | tf_op jit(solution)/shard_map/all_gather | solution.py:163
  523.5 142.0 %reduce-scatter.5.cloned.1.call-start = ((), (), s32[]{:S(2)}) async-start(), calls=%async_computation.8 | async-start | bytes 3342336 | tf_op jit(solution)/shard_map/reduce_scatter | solution.py:169
  585.9 0.7 copy-start.6
  585.9 0.7 copy-start.7
  585.9 79.6 %copy-start.2 = (bf16[2,32,1536]{2,1,0:T(8,128)(2,1)S(1)}, bf16[2,32,1536]{2,1,0:T(8,128)(2,1)}, u32[]{:S(2)}) copy-start(bf16[2,32,1536]{2,1,0:T(8,128)(2,1)} %reduce-scatter.3.cloned.1.call-done) | copy-start | bytes 589828
  585.9 81.9 %copy-start.12 = (bf16[1536,64]{0,1:T(8,128)(2,1)S(1)}, bf16[1536,64]{0,1:T(8,128)(2,1)}, u32[]{:S(2)}) copy-start(bf16[1536,64]{0,1:T(8,128)(2,1)} %param.27) | copy-start | bytes 589828
  585.9 86.4 %copy-start.10 = (f32[2,32,32]{2,1,0:T(8,128)S(1)}, f32[2,32,32]{2,1,0:T(8,128)}, u32[]{:S(2)}) copy-start(f32[2,32,32]{2,1,0:T(8,128)} %param.19) | copy-start | bytes 24580
  669.1 3.3 collective-permute-start
Sparse Core Ops, SparseCore 0:
  314.2 84.2 all-gather.3
  476.7 42.7 reduce-scatter.2
  523.6 54.7 all-gather.5
  586.1 79.3 reduce-scatter.4
where the time goes:
time: 809 us
  blocking collectives  479 us (59%)
  waiting for transfers between devices  241 us (30%)
  other arithmetic  23.5 us (3%)
  local copies, waits for them, and re-layouts  21.2 us (3%)
  matrix products  21.1 us (3%)
  between operations  14 us (2%)
  starting transfers between devices  8.55 us (1%)
    all_gather x1, blocking collectives, on_device(): every_mod = lax.all_gather(columns, ('req', 'seq'), axis=1, tiled=True)  300 us
    reduce_scatter x1, waiting for transfers between devices, on_device(): lax.psum_scatter(mlp_terms.astype(jnp.bfloat16), 'seq', scatter_dimension...  78.8 us
    psum x1, blocking collectives, on_device(): square_total = lax.psum(squares, ('cfg', 'seq'))  65.3 us
    pmax x1, blocking collectives, on_device(): peak_value = lax.pmax(largest, ('cfg', 'seq'))  63.2 us
    all_gather x1, waiting for transfers between devices, on_device(): lax.all_gather(mlp_in, 'seq', axis=1, tiled=True)  54.8 us
    all_gather x1, waiting for transfers between devices, on_device(): lax.all_gather(img_in, 'req', axis=0, tiled=True)  51.1 us
    reduce_scatter x1, waiting for transfers between devices, on_device(): lax.psum_scatter(moved_rows.astype(jnp.bfloat16), 'req', scatter_dimensio...  42.2 us
    all_gather x1, blocking collectives, on_device(): lax.all_gather(txt_in, 'req', axis=0, tiled=True)  19.9 us
  transfers between devices with their start and end apart: 6, of which 6 were waited for; matrix products, arithmetic and copies ran while one was open for 0% of the time, Pallas kernels for 0%

commit v1 on v0

--- a/solution.py
+++ b/solution.py
@@ -84,6 +84,18 @@
     fc_out,
     final_weight,
 ):
+
+    def _run_lane(buf, k_dim, at_axis):
+        return jnp.concatenate(
+            lax.all_to_all(
+                jnp.stack(jnp.split(buf, lax.axis_size("seq"), axis=k_dim)),
+                axis_name="seq",
+                concat_axis=0,
+                split_axis=0,
+            ),
+            axis=at_axis,
+        )
+
     group_size = img_hidden.shape[1]
     current, upcoming = plan(timestep)
     activated = jax.nn.silu(pooled[0] + time_features(current)).astype(jnp.bfloat16)
@@ -150,9 +162,7 @@
     projected_rows = jnp.einsum(
         "rnk,kd->rnd", attended, out_weight, preferred_element_type=jnp.float32
     )
-    moved_rows = lax.all_to_all(
-        projected_rows.astype(jnp.bfloat16), "seq", split_axis=1, concat_axis=0, tiled=True
-    ).astype(projected_rows.dtype)
+    moved_rows = _run_lane(projected_rows.astype(jnp.bfloat16), 1, 0).astype(projected_rows.dtype)
     attn_out = lax.psum_scatter(
         moved_rows.astype(jnp.bfloat16), "req", scatter_dimension=0, tiled=True
     ).astype(jnp.float32)

time: 809 us -> 781 us (0.965)
  local copies, waits for them, and re-layouts: 21.2 us -> 3.73 us
  other arithmetic: 23.5 us -> 11.5 us
    unnamed x39 -> x40, local copies, waits for them, and re-layouts: 15.2 us -> 1.83 us
    unnamed x1 -> x0, other arithmetic: 11.5 us -> none
where the time goes in v1:
time: 781 us; the launch traced here: 780 us
  blocking collectives  479 us (61%)
  waiting for transfers between devices  242 us (31%)
  matrix products  21.1 us (3%)
  between operations  14.2 us (2%)
  other arithmetic  11.5 us (1%)
  starting transfers between devices  8.61 us (1%)
    all_gather x1, blocking collectives, on_device(): every_mod = lax.all_gather(columns, ('req', 'seq'), axis=1, tiled=True)  300 us
    reduce_scatter x1, waiting for transfers between devices, on_device(): lax.psum_scatter(mlp_terms.astype(jnp.bfloat16), 'seq', scatter_dimension...  79.5 us
    psum x1, blocking collectives, on_device(): square_total = lax.psum(squares, ('cfg', 'seq'))  65.3 us
    pmax x1, blocking collectives, on_device(): peak_value = lax.pmax(largest, ('cfg', 'seq'))  63.2 us
    all_gather x1, waiting for transfers between devices, on_device(): lax.all_gather(mlp_in, 'seq', axis=1, tiled=True)  54.8 us
    all_gather x1, waiting for transfers between devices, on_device(): lax.all_gather(img_in, 'req', axis=0, tiled=True)  50.7 us
    reduce_scatter x1, waiting for transfers between devices, on_device(): lax.psum_scatter(moved_rows.astype(jnp.bfloat16), 'req', scatter_dimensio...  42.9 us
    all_gather x1, blocking collectives, on_device(): lax.all_gather(txt_in, 'req', axis=0, tiled=True)  19.9 us
  transfers between devices with their start and end apart: 6, of which 6 were waited for; matrix products, arithmetic and copies ran while one was open for 0% of the time, Pallas kernels for 0%

profile of v1, /device:TPU:1, one launch (start us, length us, event | category | flops | bytes accessed | tf_op | source)
XLA Modules:
  0.0 780.2 jit_solution(12110324550294618476)
XLA Ops:
  7.2 0.8 divide_subtract_fusion
  8.0 0.3 multiply_cosine_fusion
  8.3 1.2 fusion.18
  9.5 299.6 %all-gather = f32[128,120,16]{1,2,0:T(8,128)S(1)} all-gather(f32[1,120,16]{1,2,0:T(8,128)S(1)} %fusion.18), channel_id=1, replica_groups=mesh['cfg'=2,'req'=8,'seq'=16] {'req','seq'}, dimensions={0}, use_global_device_ids=true | all-gather | bytes 990720 | tf_op jit(solution)/shard_map/all_gather | solution.py:103
  309.1 0.3 copy.22
  309.5 1.6 reshape.181
  311.0 1.1 dynamic-slice_bitcast_fusion
  312.1 0.1 reshape.171
  312.2 0.1 fusion.76
  312.3 0.1 convert_reduce_fusion
  312.4 0.2 fusion.31
  312.7 0.8 fusion.34
  313.5 0.1 convert_reduce_fusion.1
  313.6 0.2 fusion.39
  313.9 0.1 fusion.42
  314.0 19.9 %all_gather.14 = bf16[16,10,1536]{2,1,0:T(8,128)(2,1)S(1)} all-gather(bf16[2,10,1536]{2,1,0:T(8,128)(2,1)S(1)} %fusion.42), channel_id=1, replica_groups=mesh['cfg'=2,'req'=8,'seq'=16] {'req'}, dimensions={0}, use_global_device_ids=true | all-gather | bytes 552960 | tf_op jit(solution)/shard_map/all_gather | solution.py:119
  333.9 13.1 %all_to_all.23 = bf16[16,10,1536]{2,1,0:T(8,128)(2,1)S(1)} all-to-all(bf16[16,10,1536]{2,1,0:T(8,128)(2,1)S(1)} %all_gather.14), channel_id=1, replica_groups=mesh['cfg'=2,'req'=8,'seq'=16] {'seq'}, dimensions={0} | all-to-all | bytes 983040 | tf_op jit(solution)/shard_map/all_to_all | solution.py:127
  346.9 50.7 %all-gather.4.cloned.1.call-done = bf16[16,32,1536]{2,1,0:T(8,128)(2,1)} async-done(((bf16[2,32,1536]{2,1,0:T(8,128)(2,1)}), bf16[16,32,1536]{2,1,0:T(8,128)(2,1)}) %all-gather.4.cloned.1.call-update) | async-done | bytes 1572880 | tf_op jit(solution)/shard_map/all_gather | solution.py:118
  397.6 6.1 all-to-all-start
  403.8 0.6 fusion.78
  404.4 0.6 iota_compare_fusion
  405.0 0.2 reshape.174
  405.2 1.7 convolution_convert_fusion.3
  407.0 13.4 %all-to-all-done = bf16[16,32,1536]{2,1,0:T(8,128)(2,1)} async-done(((bf16[16,32,1536]{2,1,0:T(8,128)(2,1)}), bf16[16,32,1536]{2,1,0:T(8,128)(2,1)}, u32[]{:S(2)}, u32[]{:S(2)}) %all-to-all-start) | async-done | bytes 1572896 | tf_op jit(solution)/shard_map/all_to_all | solution.py:126
  420.4 2.5 convolution_convert_fusion.2
  423.0 3.5 fusion.79
  426.6 2.7 fusion.17
  429.3 0.6 fusion.2
  430.2 18.0 %all_to_all.24 = bf16[16,1,32,1536]{3,2,1,0:T(8,128)(2,1)} all-to-all(bf16[16,1,32,1536]{3,2,1,0:T(8,128)(2,1)S(1)} %fusion.49), channel_id=1, replica_groups=mesh['cfg'=2,'req'=8,'seq'=16] {'seq'}, dimensions={0} | all-to-all | bytes 3145728 | tf_op jit(solution)/shard_map/all_to_all | solution.py:90
  448.2 0.0 all-gather.6.cloned.1.call-start
  448.3 42.9 %reduce-scatter.3.cloned.1.call-done = bf16[2,32,1536]{2,1,0:T(8,128)(2,1)} async-done(((bf16[16,32,1536]{2,1,0:T(8,128)(2,1)}), bf16[2,32,1536]{2,1,0:T(8,128)(2,1)}) %reduce-scatter.3.cloned.1.call-update) | async-done | bytes 196624 | tf_op jit(solution)/shard_map/reduce_scatter | solution.py:166
  491.1 1.1 fusion.35
  492.2 1.1 multiply_reduce_fusion.1
  493.4 1.8 add_convert_fusion.1
  495.2 54.8 %all-gather.6.cloned.1.call-done = bf16[2,512,1536]{2,1,0:T(8,128)(2,1)} async-done(((bf16[2,32,1536]{2,1,0:T(8,128)(2,1)}), bf16[2,512,1536]{2,1,0:T(8,128)(2,1)}) %all-gather.6.cloned.1.call-update) | async-done | bytes 3145744 | tf_op jit(solution)/shard_map/all_gather | solution.py:173
  550.0 7.6 convolution_convert_fusion
  557.6 79.5 %reduce-scatter.5.cloned.1.call-done = bf16[2,32,1536]{2,1,0:T(8,128)(2,1)} async-done(((bf16[2,512,1536]{2,1,0:T(8,128)(2,1)}), bf16[2,32,1536]{2,1,0:T(8,128)(2,1)}) %reduce-scatter.5.cloned.1.call-update) | async-done | bytes 196624 | tf_op jit(solution)/shard_map/reduce_scatter | solution.py:179
  637.2 1.1 fusion.74
  638.3 1.1 multiply_reduce_fusion
  639.5 1.2 fusion.43
  640.7 0.1 constant_dynamic-slice_fusion
  640.8 2.3 collective-permute-start
  643.1 0.1 dynamic_slice.34
  643.2 0.8 collective-permute-done
  644.0 0.7 abs_reduce_fusion
  644.7 65.3 %psum.7 = f32[2]{0:T(128)S(1)} all-reduce(f32[2]{0:T(128)S(1)} %get-tuple-element.41), channel_id=1, replica_groups=mesh['cfg'=2,'req'=8,'seq'=16] {'cfg','seq'}, use_global_device_ids=true, to_apply=%region_13.14 | all-reduce | flops 2 | bytes 16 | tf_op jit(solution)/shard_map/psum | solution.py:202
  710.0 0.5 multiply_sqrt_fusion
  710.5 63.2 %pmax.7 = f32[2]{0:T(128)} all-reduce(f32[2]{0:T(128)S(1)} %get-tuple-element.40), channel_id=1, replica_groups=mesh['cfg'=2,'req'=8,'seq'=16] {'cfg','seq'}, use_global_device_ids=true, to_apply=%region_15.16 | all-reduce | flops 2 | bytes 16 | tf_op jit(solution)/shard_map/pmax | solution.py:203
  (61 shorter events, 0.7 us)
Async XLA Ops:
  7.2 413.2 %copy-start = (bf16[1536,3,192]{0,2,1:T(8,128)(2,1)S(1)}, bf16[1536,3,192]{0,2,1:T(8,128)(2,1)}, u32[]{:S(2)}) copy-start(bf16[1536,3,192]{0,2,1:T(8,128)(2,1)} %param.22) | copy-start | bytes 5308420
  7.2 390.4 %all-gather.4.cloned.1.call-start = ((), (), s32[]{:S(2)}) async-start(), calls=%async_computation.5 | async-start | bytes 1769472 | tf_op jit(solution)/shard_map/all_gather | solution.py:118
  309.4 2.9 copy-start.1
  309.4 4.1 copy-start.4
  346.9 56.9 %copy-start.8 = (s32[1,16]{1,0:T(1,128)S(1)}, s32[1,16]{1,0:T(1,128)}, u32[]{:S(2)}) copy-start(s32[1,16]{1,0:T(1,128)} %param.16) | copy-start | bytes 196
  397.6 22.8 %all-to-all-start = ((bf16[16,32,1536]{2,1,0:T(8,128)(2,1)}), bf16[16,32,1536]{2,1,0:T(8,128)(2,1)}, u32[]{:S(2)}, u32[]{:S(2)}) async-start(bf16[16,32,1536]{2,1,0:T(8,128)(2,1)} %all-gather.4.cloned.1.call-done), calls=%async_computation | async-start | bytes 3145728 | tf_op jit(solution)/shard_map/all_to_all | solution.py:126
  403.7 87.4 %reduce-scatter.3.cloned.1.call-start = ((), (), s32[]{:S(2)}) async-start(), calls=%async_computation.6 | async-start | bytes 1769472 | tf_op jit(solution)/shard_map/reduce_scatter | solution.py:166
  426.6 2.7 copy-start.3
  448.2 101.8 %copy-start.6 = (bf16[384,1536]{1,0:T(8,128)(2,1)S(1)}, bf16[384,1536]{1,0:T(8,128)(2,1)}, u32[]{:S(2)}) copy-start(bf16[384,1536]{1,0:T(8,128)(2,1)} %param.26) | copy-start | bytes 3538948
  448.2 101.8 %all-gather.6.cloned.1.call-start = ((), (), s32[]{:S(2)}) async-start(), calls=%async_computation.7 | async-start | bytes 3342336 | tf_op jit(solution)/shard_map/all_gather | solution.py:173
  495.2 142.0 %reduce-scatter.5.cloned.1.call-start = ((), (), s32[]{:S(2)}) async-start(), calls=%async_computation.8 | async-start | bytes 3342336 | tf_op jit(solution)/shard_map/reduce_scatter | solution.py:179
  557.5 79.6 %copy-start.2 = (bf16[2,32,1536]{2,1,0:T(8,128)(2,1)S(1)}, bf16[2,32,1536]{2,1,0:T(8,128)(2,1)}, u32[]{:S(2)}) copy-start(bf16[2,32,1536]{2,1,0:T(8,128)(2,1)} %reduce-scatter.3.cloned.1.call-done) | copy-start | bytes 589828
  557.5 81.9 %copy-start.7 = (bf16[1536,64]{0,1:T(8,128)(2,1)S(1)}, bf16[1536,64]{0,1:T(8,128)(2,1)}, u32[]{:S(2)}) copy-start(bf16[1536,64]{0,1:T(8,128)(2,1)} %param.27) | copy-start | bytes 589828
  557.6 86.4 %copy-start.5 = (f32[2,32,32]{2,1,0:T(8,128)S(1)}, f32[2,32,32]{2,1,0:T(8,128)}, u32[]{:S(2)}) copy-start(f32[2,32,32]{2,1,0:T(8,128)} %param.19) | copy-start | bytes 24580
  640.8 3.2 collective-permute-start
Sparse Core Ops, SparseCore 0:
  313.6 83.9 all-gather.3
  448.3 42.7 reduce-scatter.2
  495.3 54.6 all-gather.5
  557.7 79.4 reduce-scatter.4
